TPU v7x, 256 devices: a whole 4x4x8 slice. The times are simulated.
256 devices in a mesh: group: 2 (over core), dp: 16 (over y, x), tensor: 8 (over z).
Axes of the slice: x: 4, y: 4, z: 8, core: 2. Of those that a mesh axis runs over, the one named last changes fastest.
Arguments:
- stream: bfloat16 [512, 8192], P('tensor', ('group', 'dp'))
- norm_attn: bfloat16 [8192], P(('group', 'dp')), may hold values from 0.29882812 to 3
- norm_ffn: bfloat16 [8192], P(('group', 'dp')), may hold values from 0.29882812 to 3
- w_query: bfloat16 [8192, 8192], P(('group', 'dp'), 'tensor'), may hold values from -0.0625 to 0.0625
- w_keyval: bfloat16 [8192, 2048], P(('group', 'dp'), 'tensor'), may hold values from -0.0625 to 0.0625
- w_out: bfloat16 [8192, 8192], P('tensor', ('group', 'dp')), may hold values from -0.0625 to 0.0625
- w_gate: bfloat16 [8192, 28672], P(('group', 'dp'), 'tensor'), may hold values from -0.0625 to 0.0625
- w_up: bfloat16 [8192, 28672], P(('group', 'dp'), 'tensor'), may hold values from -0.0625 to 0.0625
- w_down: bfloat16 [28672, 8192], P('tensor', ('group', 'dp')), may hold values from -0.03125 to 0.03125
- cache: bfloat16 [512, 8, 256, 256], P(('group', 'dp'), 'tensor')
- lengths: int32 [512], P(('group', 'dp')), may hold values from 1 to 256, as said below
- location: int32 [512], P(('group', 'dp')), may hold values from 0 to 511, as said below
Outputs:
- updated: float32 [512, 8192], P('tensor', ('group', 'dp'))
Inputs may be any that keep to these rules, and one draw needn't show every extreme that they name: Each of the 512 slots is named by exactly one request. Slot s belongs to owner s // 16. Requests r of one aligned block of 16 (one device's requests) that share an owner have different values of location modulo 2; in every draw 2 of them share an owner. `lengths`: some slot holds 256 valid positions in every draw.
All inputs are finite; a program needn't handle non-finite values.
Results may differ from a plain program's by a relative error of at most 0.005.
The roundings to bfloat16 on the way count: a program that leaves them out, or rounds other values in their place, can miss the bound.
Values may be sent and summed in bfloat16 or wider, within the bound.
No kernel may reach another device: no remote copies, remote signals or barrier semaphores. Data moves between devices by JAX's collectives and lax.ppermute only.
A program may use at most 64 MiB of HBM per device.

v0:
```python
import jax
import jax.numpy as jnp
from jax import lax
from jax.sharding import PartitionSpec as P

D = 8192
WIDTH = ("group", "dp")
EPSILON = 1e-05


def gather_width(values):
    owners = lax.axis_size(WIDTH)
    sent = jnp.broadcast_to(values[None], (owners,) + values.shape)
    return lax.all_to_all(sent, WIDTH, 0, 0, tiled=True)


def scale_rows(values, squares, gain):
    scale = lax.rsqrt(squares / D + EPSILON)
    return (values * scale[:, None] * gain.astype(jnp.float32)[None, :]).astype(jnp.bfloat16)


def gather_rows(values):
    chips = lax.axis_size("dp")
    across = lax.all_to_all(
        jnp.broadcast_to(values[None], (chips,) + values.shape), "dp", 0, 0, tiled=True
    )
    cores = lax.axis_size("group")
    both = lax.all_to_all(
        jnp.broadcast_to(across[None], (cores,) + across.shape), "group", 0, 0, tiled=True
    )
    return both.reshape((-1,) + values.shape[1:])


def reduce_chips(partial, link_type):
    chips = lax.axis_size("dp")
    blocks = partial.reshape((chips, partial.shape[0] // chips) + partial.shape[1:])
    moved = lax.all_to_all(blocks.astype(link_type), "dp", 0, 0, tiled=True)
    return jnp.sum(moved.astype(jnp.float32), axis=0)


def chip_blocks(values):
    cores = lax.axis_size("group")
    parts = lax.axis_size("tensor")
    sent = jnp.broadcast_to(values[None], (cores * parts,) + values.shape)
    got = lax.all_to_all(sent, ("group", "tensor"), 0, 0, tiled=True)
    return got.reshape((cores, parts) + values.shape)


def chip_rows(values):
    blocks = chip_blocks(values)
    cores, parts, rows, width = blocks.shape
    return blocks.transpose(1, 2, 0, 3).reshape(parts * rows, cores * width)


def chip_weights(matrices):
    return lax.all_gather(jnp.concatenate(matrices, axis=1), "group", axis=0, tiled=True)


def reduce_rows(partial, axis):
    parts = lax.axis_size(axis)
    blocks = partial.reshape((parts, partial.shape[0] // parts) + partial.shape[1:])
    return jnp.sum(lax.all_to_all(blocks, axis, 0, 0, tiled=True), axis=0)


def attend(query, fresh, stored, counts):
    items = query.shape[0]
    kv_local = stored.shape[1]
    head_size = stored.shape[3] // 2
    grouped = query.reshape(items, kv_local, -1, head_size)
    fresh = fresh.reshape(items, kv_local, 2 * head_size)
    scale = head_size ** (-0.5)
    scores = (
        jnp.einsum(
            "mkgd,mkpd->mkgp", grouped, stored[..., :head_size], preferred_element_type=jnp.float32
        )
        * scale
    )
    own = (
        jnp.einsum(
            "mkgd,mkd->mkg", grouped, fresh[..., :head_size], preferred_element_type=jnp.float32
        )
        * scale
    )
    place = jnp.arange(stored.shape[2], dtype=jnp.int32)
    valid = place[None, None, None, :] < counts[:, None, None, None]
    top = jnp.maximum(jnp.max(jnp.where(valid, scores, -1e30), axis=3), own)
    expo = jnp.where(valid, jnp.exp(scores - top[..., None]), 0.0)
    own_expo = jnp.exp(own - top)
    total = jnp.sum(expo, axis=3) + own_expo
    probs = (expo / total[..., None]).astype(jnp.bfloat16)
    own_prob = (own_expo / total).astype(jnp.bfloat16)
    mixed = jnp.einsum(
        "mkgp,mkpd->mkgd", probs, stored[..., head_size:], preferred_element_type=jnp.float32
    )
    mixed = mixed + own_prob.astype(jnp.float32)[..., None] * fresh[:, :, None, head_size:].astype(
        jnp.float32
    )
    return mixed.reshape(items, -1).astype(jnp.bfloat16)


def per_device(
    stream,
    norm_attn,
    norm_ffn,
    w_query,
    w_keyval,
    w_out,
    w_gate,
    w_up,
    w_down,
    cache,
    lengths,
    location,
):
    rows = stream.shape[0]
    resid = stream.astype(jnp.float32)
    width = stream.shape[1]
    parts = lax.axis_size("tensor")
    per_owner = location.shape[0]
    pieces = jnp.concatenate([location // per_owner, location % per_owner]).astype(jnp.bfloat16)
    extra = jnp.zeros((width,), jnp.bfloat16).at[: 2 * per_owner].set(pieces)
    blocks = chip_blocks(jnp.concatenate([stream, norm_attn[None, :], extra[None, :]], axis=0))
    cores = blocks.shape[0]
    raw = blocks[:, :, :rows].transpose(1, 2, 0, 3).reshape(parts * rows, cores * width)
    raw = raw.astype(jnp.float32)
    gain = blocks[:, 0, rows].reshape(-1)
    halves = (
        blocks[:, 0, rows + 1, : 2 * per_owner].astype(jnp.float32).reshape(cores, 2, per_owner)
    )
    chip_where = halves[:, 0] * per_owner + halves[:, 1]
    chip_squares = jnp.sum(raw * raw, axis=1)
    chips = lax.axis_size("dp")
    payload = jnp.concatenate([chip_squares, chip_where.reshape(-1)])
    shared = lax.all_to_all(
        jnp.broadcast_to(payload[None], (chips, payload.shape[0])), "dp", 0, 0, tiled=True
    )
    requests = chip_squares.shape[0]
    all_squares = jnp.sum(shared[:, :requests], axis=0)
    where = shared[:, requests:].reshape(chips, cores, per_owner).transpose(1, 0, 2)
    where = where.reshape(-1).astype(jnp.int32)
    by_slot = jnp.zeros((requests,), jnp.int32).at[where].set(jnp.arange(requests, dtype=jnp.int32))
    core = lax.axis_index("group")
    half = requests // lax.axis_size("group")
    qkv_weights = chip_weights((w_query, w_keyval))
    ffn_weights = chip_weights((w_gate, w_up))
    mine = lax.dynamic_slice_in_dim(by_slot, core * half, half)
    gathered = scale_rows(raw[mine], all_squares[mine], gain)
    joined = jnp.dot(gathered, qkv_weights, preferred_element_type=jnp.float32)
    summed = reduce_chips(joined, jnp.float32)
    query_cols = w_query.shape[1]
    query = summed[:, :query_cols].astype(jnp.bfloat16)
    fresh = summed[:, query_cols:].astype(jnp.bfloat16)
    answer = attend(query, fresh, cache, lengths)
    attended = gather_rows(answer)
    mixed = jnp.dot(attended, w_out, preferred_element_type=jnp.float32)[where]
    middle = resid + reduce_rows(mixed, "tensor")
    squares = jnp.sum(gather_width(jnp.sum(middle * middle, axis=1)), axis=0)
    ffn_in = scale_rows(middle, squares, norm_ffn)
    gathered = lax.dynamic_slice_in_dim(chip_rows(ffn_in), core * half, half)
    both = reduce_chips(
        jnp.dot(gathered, ffn_weights, preferred_element_type=jnp.float32), jnp.bfloat16
    )
    hidden_cols = w_gate.shape[1]
    hidden = (jax.nn.silu(both[:, :hidden_cols]) * both[:, hidden_cols:]).astype(jnp.bfloat16)
    hidden = gather_rows(hidden)
    down = jnp.dot(hidden, w_down, preferred_element_type=jnp.float32)
    return middle + reduce_rows(down, "tensor")


def solution(mesh):
    placed = (
        P("tensor", WIDTH),
        P(WIDTH),
        P(WIDTH),
        P(WIDTH, "tensor"),
        P(WIDTH, "tensor"),
        P("tensor", WIDTH),
        P(WIDTH, "tensor"),
        P(WIDTH, "tensor"),
        P("tensor", WIDTH),
        P(WIDTH, "tensor", None, None),
        P(WIDTH),
        P(WIDTH),
    )
    return jax.shard_map(
        per_device, mesh=mesh, in_specs=placed, out_specs=P("tensor", WIDTH), check_vma=False
    )
```

profile of v0, /device:TPU:1, one launch (start us, length us, event | category | flops | bytes accessed | tf_op | source)
XLA Modules:
  0.0 287.4 jit_solution(8751193857991613794)
XLA Ops:
  6.5 2.1 pad_maximum_fusion.1
  11.8 10.0 %all-to-all-start = ((bf16[16,66,256]{2,1,0:T(8,128)(2,1)}), bf16[16,66,256]{2,1,0:T(8,128)(2,1)S(1)}, u32[]{:S(2)}, u32[]{:S(2)}) async-start(bf16[16,66,256]{2,1,0:T(8,128)(2,1)} %broadcast_in_dim.40), calls=%async_computation | async-start | bytes 1179648 | tf_op jit(solution)/shard_map/all_to_all | solution.py:45
  21.8 4.3 %pad_maximum_fusion = bf16[256,7168]{1,0:T(8,128)(2,1)} fusion(bf16[256,3584]{1,0:T(8,128)(2,1)} %param.21, bf16[256,3584]{1,0:T(8,128)(2,1)} %param.20), kind=kLoop, calls=%fused_computation.6 | loop fusion | flops 7340032 | bytes 7340032 | tf_op jit(solution)/shard_map/concatenate | solution.py:56
  26.2 11.5 %all-to-all-done = bf16[16,66,256]{2,1,0:T(8,128)(2,1)S(1)} async-done(((bf16[16,66,256]{2,1,0:T(8,128)(2,1)}), bf16[16,66,256]{2,1,0:T(8,128)(2,1)S(1)}, u32[]{:S(2)}, u32[]{:S(2)}) %all-to-all-start) | async-done | bytes 540704 | tf_op jit(solution)/shard_map/all_to_all | solution.py:45
  39.1 6.8 %all-to-all-start.1 = ((f32[16,1,544]{2,1,0:T(1,128)}), f32[16,1,544]{2,1,0:T(1,128)S(1)}, u32[]{:S(2)}, u32[]{:S(2)}) async-start(f32[16,1,544]{2,1,0:T(1,128)} %broadcast_in_dim.41), calls=%async_computation.1 | async-start | bytes 81920 | tf_op jit(solution)/shard_map/all_to_all | solution.py:134
  46.5 5.8 %all-to-all-done.1 = f32[16,1,544]{2,1,0:T(1,128)S(1)} async-done(((f32[16,1,544]{2,1,0:T(1,128)}), f32[16,1,544]{2,1,0:T(1,128)S(1)}, u32[]{:S(2)}, u32[]{:S(2)}) %all-to-all-start.1) | async-done | bytes 34848 | tf_op jit(solution)/shard_map/all_to_all | solution.py:134
  52.5 2.4 scatter_custom_fusion
  56.1 1.9 gather_fusion.1
  58.1 3.0 %fusion.4 = f32[256,1280]{1,0:T(8,128)} fusion(bf16[512,1280]{1,0:T(8,128)(2,1)} %all-gather.3.cloned.1.call-done, f32[256,512]{1,0:T(8,128)S(1)} %gather_fusion, f32[512]{0:T(512)S(1)} %bitcast.94, f32[256]{0:T(256)S(1)} %add_rsqrt_fusion), kind=kOutput, calls=%fused_computation.20 | convolution fusion | flops 335937536 | bytes 3148800 | tf_op jit(solution)/shard_map/dot_general | solution.py:148
  61.1 3.8 %all-to-all-start.2 = ((f32[16,16,1280]{2,1,0:T(8,128)}), f32[16,16,1280]{2,1,0:T(8,128)S(1)}, u32[]{:S(2)}, u32[]{:S(2)}) async-start(f32[16,16,1280]{2,1,0:T(8,128)} %bitcast.7), calls=%async_computation.2 | async-start | bytes 2621440 | tf_op jit(solution)/shard_map/all_to_all | solution.py:37
  65.0 17.3 %all-to-all-done.2 = f32[16,16,1280]{2,1,0:T(8,128)S(1)} async-done(((f32[16,16,1280]{2,1,0:T(8,128)}), f32[16,16,1280]{2,1,0:T(8,128)S(1)}, u32[]{:S(2)}, u32[]{:S(2)}) %all-to-all-start.2) | async-done | bytes 1310752 | tf_op jit(solution)/shard_map/all_to_all | solution.py:37
  82.6 1.7 select_reduce_fusion
  86.9 5.4 %all-to-all-start.3 = ((bf16[16,16,1024]{2,1,0:T(8,128)(2,1)}), bf16[16,16,1024]{2,1,0:T(8,128)(2,1)S(1)}, u32[]{:S(2)}, u32[]{:S(2)}) async-start(bf16[16,16,1024]{2,1,0:T(8,128)(2,1)} %broadcast_in_dim.45), calls=%async_computation.3 | async-start | bytes 1048576 | tf_op jit(solution)/shard_map/all_to_all | solution.py:24
  92.4 9.5 %all-to-all-done.3 = bf16[16,16,1024]{2,1,0:T(8,128)(2,1)S(1)} async-done(((bf16[16,16,1024]{2,1,0:T(8,128)(2,1)}), bf16[16,16,1024]{2,1,0:T(8,128)(2,1)S(1)}, u32[]{:S(2)}, u32[]{:S(2)}) %all-to-all-start.3) | async-done | bytes 524320 | tf_op jit(solution)/shard_map/all_to_all | solution.py:24
  102.0 7.2 %all_to_all.65 = bf16[2,16,16,1024]{3,2,1,0:T(8,128)(2,1)S(1)} all-to-all(bf16[2,16,16,1024]{3,2,1,0:T(8,128)(2,1)S(1)} %broadcast_in_dim.46), channel_id=1, replica_groups=mesh['group'=2,'dp'=16,'tensor'=8] {'group'}, dimensions={0} | all-to-all | bytes 2097152 | tf_op jit(solution)/shard_map/all_to_all | solution.py:28
  111.3 22.7 %all_to_all.66 = f32[8,64,256]{2,1,0:T(8,128)S(1)} all-to-all(f32[8,64,256]{2,1,0:T(8,128)S(1)} %bitcast.78), channel_id=1, replica_groups=mesh['group'=2,'dp'=16,'tensor'=8] {'tensor'}, dimensions={0} | all-to-all | bytes 1048576 | tf_op jit(solution)/shard_map/all_to_all | solution.py:62
  134.7 5.3 %all-to-all-start.6 = ((f32[32,1,64]{2,1,0:T(1,128)}), f32[32,1,64]{2,1,0:T(1,128)S(1)}, u32[]{:S(2)}, u32[]{:S(2)}) async-start(f32[32,1,64]{2,1,0:T(1,128)} %broadcast_in_dim.47), calls=%async_computation.6 | async-start | bytes 32768 | tf_op jit(solution)/shard_map/all_to_all | solution.py:14
  140.1 6.7 %all-to-all-done.6 = f32[32,1,64]{2,1,0:T(1,128)S(1)} async-done(((f32[32,1,64]{2,1,0:T(1,128)}), f32[32,1,64]{2,1,0:T(1,128)S(1)}, u32[]{:S(2)}, u32[]{:S(2)}) %all-to-all-start.6) | async-done | bytes 8224 | tf_op jit(solution)/shard_map/all_to_all | solution.py:14
  147.0 18.0 %all_to_all.67 = bf16[16,64,256]{2,1,0:T(8,128)(2,1)S(1)} all-to-all(bf16[16,64,256]{2,1,0:T(8,128)(2,1)S(1)} %broadcast_in_dim.48), channel_id=1, replica_groups=mesh['group'=2,'dp'=16,'tensor'=8] {'group','tensor'}, dimensions={0} | all-to-all | bytes 1048576 | tf_op jit(solution)/shard_map/all_to_all | solution.py:45
  165.6 5.2 %convolution_convert_fusion = bf16[256,7168]{1,0:T(8,128)(2,1)S(1)} fusion(bf16[512,7168]{1,0:T(8,128)(2,1)} %all-gather.5.cloned.1.call-done, bf16[512,512]{1,0:T(8,128)(2,1)S(1)} %bitcast.83, s32[]{:T(128)S(6)} %select_n.43), kind=kOutput, calls=%fused_computation.4 | convolution fusion | flops 1880883200 | bytes 11272196 | tf_op jit(solution)/shard_map/dot_general | solution.py:161
  170.8 46.8 %all_to_all.68 = bf16[16,16,7168]{2,1,0:T(8,128)(2,1)S(1)} all-to-all(bf16[16,16,7168]{2,1,0:T(8,128)(2,1)S(1)} %bitcast.76), channel_id=1, replica_groups=mesh['group'=2,'dp'=16,'tensor'=8] {'dp'}, dimensions={0} | all-to-all | bytes 7340032 | tf_op jit(solution)/shard_map/all_to_all | solution.py:37
  218.4 26.6 %all_to_all.69 = bf16[16,16,3584]{2,1,0:T(8,128)(2,1)S(1)} all-to-all(bf16[16,16,3584]{2,1,0:T(8,128)(2,1)S(1)} %broadcast_in_dim.49), channel_id=1, replica_groups=mesh['group'=2,'dp'=16,'tensor'=8] {'dp'}, dimensions={0} | all-to-all | bytes 3670016 | tf_op jit(solution)/shard_map/all_to_all | solution.py:24
  245.4 9.5 %all_to_all.70 = bf16[2,16,16,3584]{3,2,1,0:T(8,128)(2,1)S(1)} all-to-all(bf16[2,16,16,3584]{3,2,1,0:T(8,128)(2,1)S(1)} %broadcast_in_dim.50), channel_id=1, replica_groups=mesh['group'=2,'dp'=16,'tensor'=8] {'group'}, dimensions={0} | all-to-all | bytes 7340032 | tf_op jit(solution)/shard_map/all_to_all | solution.py:28
  256.0 23.8 %all_to_all.71 = f32[8,64,256]{2,1,0:T(8,128)S(1)} all-to-all(f32[8,64,256]{2,1,0:T(8,128)S(1)} %fusion), channel_id=1, replica_groups=mesh['group'=2,'dp'=16,'tensor'=8] {'tensor'}, dimensions={0} | all-to-all | bytes 1048576 | tf_op jit(solution)/shard_map/all_to_all | solution.py:62
  (81 shorter events, 16.1 us)
Async XLA Ops:
  6.5 248.4 %copy-start = (bf16[3584,256]{1,0:T(8,128)(2,1)S(1)}, bf16[3584,256]{1,0:T(8,128)(2,1)}, u32[]{:S(2)}) copy-start(bf16[3584,256]{1,0:T(8,128)(2,1)} %param.22) | copy-start | bytes 5505028
  6.5 51.5 %all-gather.3.cloned.1.call-start = ((), (), s32[]{:S(2)}) async-start(), calls=%async_computation.12 | async-start | bytes 1966080 | tf_op jit(solution)/shard_map/all_gather | solution.py:56
  11.8 25.9 %all-to-all-start = ((bf16[16,66,256]{2,1,0:T(8,128)(2,1)}), bf16[16,66,256]{2,1,0:T(8,128)(2,1)S(1)}, u32[]{:S(2)}, u32[]{:S(2)}) async-start(bf16[16,66,256]{2,1,0:T(8,128)(2,1)} %broadcast_in_dim.40), calls=%async_computation | async-start | bytes 1179648 | tf_op jit(solution)/shard_map/all_to_all | solution.py:45
  21.8 143.9 %all-gather.5.cloned.1.call-start = ((), (), s32[]{:S(2)}) async-start(), calls=%async_computation.13 | async-start | bytes 11010048 | tf_op jit(solution)/shard_map/all_gather | solution.py:56
  39.1 13.2 %all-to-all-start.1 = ((f32[16,1,544]{2,1,0:T(1,128)}), f32[16,1,544]{2,1,0:T(1,128)S(1)}, u32[]{:S(2)}, u32[]{:S(2)}) async-start(f32[16,1,544]{2,1,0:T(1,128)} %broadcast_in_dim.41), calls=%async_computation.1 | async-start | bytes 81920 | tf_op jit(solution)/shard_map/all_to_all | solution.py:134
  61.1 3.8 %copy-start.3 = (s32[16]{0:T(128)S(1)}, s32[16]{0:T(128)}, u32[]{:S(2)}) copy-start(s32[16]{0:T(128)} %param.24) | copy-start | bytes 196
  61.1 21.2 %all-to-all-start.2 = ((f32[16,16,1280]{2,1,0:T(8,128)}), f32[16,16,1280]{2,1,0:T(8,128)S(1)}, u32[]{:S(2)}, u32[]{:S(2)}) async-start(f32[16,16,1280]{2,1,0:T(8,128)} %bitcast.7), calls=%async_computation.2 | async-start | bytes 2621440 | tf_op jit(solution)/shard_map/all_to_all | solution.py:37
  86.9 15.0 %all-to-all-start.3 = ((bf16[16,16,1024]{2,1,0:T(8,128)(2,1)}), bf16[16,16,1024]{2,1,0:T(8,128)(2,1)S(1)}, u32[]{:S(2)}, u32[]{:S(2)}) async-start(bf16[16,16,1024]{2,1,0:T(8,128)(2,1)} %broadcast_in_dim.45), calls=%async_computation.3 | async-start | bytes 1048576 | tf_op jit(solution)/shard_map/all_to_all | solution.py:24
  92.3 16.9 %copy-start.2 = (bf16[1024,256]{1,0:T(8,128)(2,1)S(1)}, bf16[1024,256]{1,0:T(8,128)(2,1)}, u32[]{:S(2)}) copy-start(bf16[1024,256]{1,0:T(8,128)(2,1)} %param.19) | copy-start | bytes 1572868
  109.7 24.3 %copy-start.1 = (bf16[64,256]{1,0:T(8,128)(2,1)S(1)}, bf16[64,256]{1,0:T(8,128)(2,1)}, u32[]{:S(2)}) copy-start(bf16[64,256]{1,0:T(8,128)(2,1)} %param.14) | copy-start | bytes 98308
  109.7 30.4 %copy-start.4 = (bf16[256]{0:T(256)(128)(2,1)S(1)}, bf16[256]{0:T(256)(128)(2,1)}, u32[]{:S(2)}) copy-start(bf16[256]{0:T(256)(128)(2,1)} %param.16) | copy-start | bytes 1540
  134.7 12.1 %all-to-all-start.6 = ((f32[32,1,64]{2,1,0:T(1,128)}), f32[32,1,64]{2,1,0:T(1,128)S(1)}, u32[]{:S(2)}, u32[]{:S(2)}) async-start(f32[32,1,64]{2,1,0:T(1,128)} %broadcast_in_dim.47), calls=%async_computation.6 | async-start | bytes 32768 | tf_op jit(solution)/shard_map/all_to_all | solution.py:14
Sparse Core Ops, SparseCore 0:
  9.1 19.2 all-gather.2
  30.2 24.9 all-gather.4
where the time goes:
time: 288 us; the launch traced here: 287 us
  blocking collectives  155 us (54%)
  waiting for transfers between devices  51 us (18%)
  starting transfers between devices  31.3 us (11%)
  between operations  13.8 us (5%)
  local copies, waits for them, and re-layouts  13.3 us (5%)
  matrix products  13.1 us (5%)
  other arithmetic  10.4 us (4%)
    all_to_all x1, blocking collectives, reduce_chips(): moved = lax.all_to_all(blocks.astype(link_type), 'dp', 0, 0, tiled=True)  46.8 us
    all_to_all x2, blocking collectives, reduce_rows(): return jnp.sum(lax.all_to_all(blocks, axis, 0, 0, tiled=True), axis=0)  46.5 us
    all_to_all x1, blocking collectives, gather_rows(): lax.all_to_all(jnp.broadcast_to(values[None], (chips,) + values.shape), '...  26.6 us
    all_to_all x1, blocking collectives, chip_blocks(): got = lax.all_to_all(sent, ('group', 'tensor'), 0, 0, tiled=True)  18 us
    all_to_all x1, waiting for transfers between devices, reduce_chips(): moved = lax.all_to_all(blocks.astype(link_type), 'dp', 0, 0, tiled=True)  17.3 us
    all_to_all x2, blocking collectives, gather_rows(): lax.all_to_all(jnp.broadcast_to(across[None], (cores,) + across.shape), '...  16.7 us
    all_to_all x1, waiting for transfers between devices, chip_blocks(): got = lax.all_to_all(sent, ('group', 'tensor'), 0, 0, tiled=True)  11.5 us
    all_to_all x1, starting transfers between devices, chip_blocks(): got = lax.all_to_all(sent, ('group', 'tensor'), 0, 0, tiled=True)  9.97 us
  transfers between devices with their start and end apart: 7, of which 5 were waited for; matrix products, arithmetic and copies ran while one was open for 9% of the time, Pallas kernels for 0%

commit v1 on v0

--- a/solution.py
+++ b/solution.py
@@ -6,6 +6,29 @@
 D = 8192
 WIDTH = ("group", "dp")
 EPSILON = 1e-05
+
+
+def cut_along(array, dim, length):
+    lengths = array.shape
+    blocks = array.reshape(*lengths[:dim], length, lengths[dim] // length, *lengths[dim + 1 :])
+    return jnp.moveaxis(blocks, dim, 0)
+
+
+def laid_out(blocks, dim):
+    dims = list(blocks.shape[1:])
+    dims[dim] *= blocks.shape[0]
+    return jnp.moveaxis(blocks, 0, dim).reshape(dims)
+
+
+def swapped_with_each(x, axis, split_dim, concat_dim):
+    size, position = (lax.axis_size(axis), lax.axis_index(axis))
+    tiles = cut_along(x, split_dim, size)
+    outs = [tiles[position]]
+    for step in range(1, size):
+        sent = tiles[position ^ step]
+        outs.append(lax.ppermute(sent, axis, [(i, i ^ step) for i in range(size)]))
+    tiles = jnp.stack(outs)[position ^ jnp.arange(size)]
+    return laid_out(tiles, concat_dim)
 
 
 def gather_width(values):
@@ -42,7 +65,7 @@
     cores = lax.axis_size("group")
     parts = lax.axis_size("tensor")
     sent = jnp.broadcast_to(values[None], (cores * parts,) + values.shape)
-    got = lax.all_to_all(sent, ("group", "tensor"), 0, 0, tiled=True)
+    got = swapped_with_each(sent, ("group", "tensor"), 0, 0)
     return got.reshape((cores, parts) + values.shape)
 
 

time: 288 us -> 374 us (1.30)
  starting transfers between devices: 31.3 us -> 87.3 us
  waiting for transfers between devices: 51 us -> 95 us
  blocking collectives: 155 us -> 135 us
    ppermute x0 -> x30, starting transfers between devices: none -> 66.9 us  [swapped_with_each(): outs.append(lax.ppermute(sent, axis, [(i, i ^ step) for i in range(size)]))]
    ppermute x0 -> x30, waiting for transfers between devices: none -> 60.8 us  [swapped_with_each(): outs.append(lax.ppermute(sent, axis, [(i, i ^ step) for i in range(size)]))]
    all_to_all x1 -> x0, blocking collectives: 18 us -> none  [chip_blocks(): got = lax.all_to_all(sent, ('group', 'tensor'), 0, 0, tiled=True)]
    all_to_all x1 -> x0, waiting for transfers between devices: 11.5 us -> none  [chip_blocks(): got = lax.all_to_all(sent, ('group', 'tensor'), 0, 0, tiled=True)]
    all_to_all x1 -> x0, starting transfers between devices: 9.97 us -> none  [chip_blocks(): got = lax.all_to_all(sent, ('group', 'tensor'), 0, 0, tiled=True)]
    all_to_all x1, waiting for transfers between devices: 17.3 us -> 13 us  [reduce_chips(): moved = lax.all_to_all(blocks.astype(link_type), 'dp', 0, 0, tiled=True)]
  transfers between devices with their start and end apart: 7 -> 36, of which waited for: 5 -> 25; matrix products, arithmetic and copies ran while one was open for 9% -> 7% of each run, Pallas kernels for 0% -> 0%
where the time goes in v1:
time: 374 us; the launch traced here: 373 us
  blocking collectives  135 us (36%)
  waiting for transfers between devices  95 us (25%)
  starting transfers between devices  87.3 us (23%)
  local copies, waits for them, and re-layouts  14.9 us (4%)
  between operations  13.9 us (4%)
  other arithmetic  13.5 us (4%)
  matrix products  13.3 us (4%)
    ppermute x30, starting transfers between devices, swapped_with_each(): outs.append(lax.ppermute(sent, axis, [(i, i ^ step) for i in range(size)]))  66.9 us
    ppermute x30, waiting for transfers between devices, swapped_with_each(): outs.append(lax.ppermute(sent, axis, [(i, i ^ step) for i in range(size)]))  60.8 us
    all_to_all x1, blocking collectives, reduce_chips(): moved = lax.all_to_all(blocks.astype(link_type), 'dp', 0, 0, tiled=True)  47.3 us
    all_to_all x2, blocking collectives, reduce_rows(): return jnp.sum(lax.all_to_all(blocks, axis, 0, 0, tiled=True), axis=0)  44 us
    all_to_all x1, blocking collectives, gather_rows(): lax.all_to_all(jnp.broadcast_to(values[None], (chips,) + values.shape), '...  27.2 us
    all_to_all x2, blocking collectives, gather_rows(): lax.all_to_all(jnp.broadcast_to(across[None], (cores,) + across.shape), '...  16.2 us
    all_to_all x1, waiting for transfers between devices, reduce_chips(): moved = lax.all_to_all(blocks.astype(link_type), 'dp', 0, 0, tiled=True)  13 us
    all_to_all x1, waiting for transfers between devices, gather_rows(): lax.all_to_all(jnp.broadcast_to(values[None], (chips,) + values.shape), '...  9.29 us
  transfers between devices with their start and end apart: 36, of which 25 were waited for; matrix products, arithmetic and copies ran while one was open for 7% of the time, Pallas kernels for 0%

profile of v1, /device:TPU:1, one launch (start us, length us, event | category | flops | bytes accessed | tf_op | source)
XLA Modules:
  0.0 372.7 jit_solution(13926027872821718137)
XLA Ops:
  8.8 7.0 %collective-permute-start.14 = (bf16[1,66,256]{2,1,0:T(8,128)(2,1)S(1)}, bf16[1,66,256]{2,1,0:T(8,128)(2,1)S(1)}, u32[]{:S(2)}, u32[]{:S(2)}) collective-permute-start(bf16[1,66,256]{2,1,0:T(8,128)(2,1)S(1)} %fusion.14), channel_id=1, source_target_pairs={{0,135},{1,134},{2,133},{3,132},{4,131},{5,130},{6,129},{7,128},{1... | collective-permute-start | bytes 101384 | tf_op jit(solution)/shard_map/ppermute | solution.py:29
  42.4 5.5 %collective-permute-done.4 = bf16[1,66,256]{2,1,0:T(8,128)(2,1)S(1)} collective-permute-done((bf16[1,66,256]{2,1,0:T(8,128)(2,1)S(1)}, bf16[1,66,256]{2,1,0:T(8,128)(2,1)S(1)}, u32[]{:S(2)}, u32[]{:S(2)}) %collective-permute-start.4) | collective-permute-done | bytes 33824 | tf_op jit(solution)/shard_map/ppermute | solution.py:29
  47.9 4.9 %collective-permute-done.5 = bf16[1,66,256]{2,1,0:T(8,128)(2,1)S(1)} collective-permute-done((bf16[1,66,256]{2,1,0:T(8,128)(2,1)S(1)}, bf16[1,66,256]{2,1,0:T(8,128)(2,1)S(1)}, u32[]{:S(2)}, u32[]{:S(2)}) %collective-permute-start.5) | collective-permute-done | bytes 33824 | tf_op jit(solution)/shard_map/ppermute | solution.py:29
  57.3 6.4 %collective-permute-start.7 = (bf16[1,66,256]{2,1,0:T(8,128)(2,1)S(1)}, bf16[1,66,256]{2,1,0:T(8,128)(2,1)S(1)}, u32[]{:S(2)}, u32[]{:S(2)}) collective-permute-start(bf16[1,66,256]{2,1,0:T(8,128)(2,1)S(1)} %fusion.14), channel_id=1, source_target_pairs={{0,128},{1,129},{2,130},{3,131},{4,132},{5,133},{6,134},{7,135},{1... | collective-permute-start | bytes 101384 | tf_op jit(solution)/shard_map/ppermute | solution.py:29
  82.1 6.8 %all-to-all-start = ((f32[16,1,544]{2,1,0:T(1,128)}), f32[16,1,544]{2,1,0:T(1,128)S(1)}, u32[]{:S(2)}, u32[]{:S(2)}) async-start(f32[16,1,544]{2,1,0:T(1,128)} %broadcast_in_dim.36), calls=%async_computation | async-start | bytes 81920 | tf_op jit(solution)/shard_map/all_to_all | solution.py:157
  90.2 5.1 %all-to-all-done = f32[16,1,544]{2,1,0:T(1,128)S(1)} async-done(((f32[16,1,544]{2,1,0:T(1,128)}), f32[16,1,544]{2,1,0:T(1,128)S(1)}, u32[]{:S(2)}, u32[]{:S(2)}) %all-to-all-start) | async-done | bytes 34848 | tf_op jit(solution)/shard_map/all_to_all | solution.py:157
  107.7 4.3 %pad_maximum_fusion = bf16[256,7168]{1,0:T(8,128)(2,1)} fusion(bf16[256,3584]{1,0:T(8,128)(2,1)} %param.21, bf16[256,3584]{1,0:T(8,128)(2,1)} %param.20), kind=kLoop, calls=%fused_computation.8 | loop fusion | flops 7340032 | bytes 7340032 | tf_op jit(solution)/shard_map/concatenate | solution.py:79
  112.8 13.0 %all-to-all-done.1 = f32[16,16,1280]{2,1,0:T(8,128)S(1)} async-done(((f32[16,16,1280]{2,1,0:T(8,128)}), f32[16,16,1280]{2,1,0:T(8,128)S(1)}, u32[]{:S(2)}, u32[]{:S(2)}) %all-to-all-start.1) | async-done | bytes 1310752 | tf_op jit(solution)/shard_map/all_to_all | solution.py:60
  130.7 4.5 %all-to-all-start.2 = ((bf16[16,16,1024]{2,1,0:T(8,128)(2,1)}), bf16[16,16,1024]{2,1,0:T(8,128)(2,1)S(1)}, u32[]{:S(2)}, u32[]{:S(2)}) async-start(bf16[16,16,1024]{2,1,0:T(8,128)(2,1)} %broadcast_in_dim.40), calls=%async_computation.2 | async-start | bytes 1048576 | tf_op jit(solution)/shard_map/all_to_all | solution.py:47
  135.2 9.3 %all-to-all-done.2 = bf16[16,16,1024]{2,1,0:T(8,128)(2,1)S(1)} async-done(((bf16[16,16,1024]{2,1,0:T(8,128)(2,1)}), bf16[16,16,1024]{2,1,0:T(8,128)(2,1)S(1)}, u32[]{:S(2)}, u32[]{:S(2)}) %all-to-all-start.2) | async-done | bytes 524320 | tf_op jit(solution)/shard_map/all_to_all | solution.py:47
  144.6 7.4 %all_to_all.55 = bf16[2,16,16,1024]{3,2,1,0:T(8,128)(2,1)S(1)} all-to-all(bf16[2,16,16,1024]{3,2,1,0:T(8,128)(2,1)S(1)} %broadcast_in_dim.41), channel_id=1, replica_groups=mesh['group'=2,'dp'=16,'tensor'=8] {'group'}, dimensions={0} | all-to-all | bytes 2097152 | tf_op jit(solution)/shard_map/all_to_all | solution.py:51
  154.1 24.6 %all_to_all.56 = f32[8,64,256]{2,1,0:T(8,128)S(1)} all-to-all(f32[8,64,256]{2,1,0:T(8,128)S(1)} %bitcast.147), channel_id=1, replica_groups=mesh['group'=2,'dp'=16,'tensor'=8] {'tensor'}, dimensions={0} | all-to-all | bytes 1048576 | tf_op jit(solution)/shard_map/all_to_all | solution.py:85
  179.6 5.3 %all-to-all-start.5 = ((f32[32,1,64]{2,1,0:T(1,128)}), f32[32,1,64]{2,1,0:T(1,128)S(1)}, u32[]{:S(2)}, u32[]{:S(2)}) async-start(f32[32,1,64]{2,1,0:T(1,128)} %broadcast_in_dim.42), calls=%async_computation.5 | async-start | bytes 32768 | tf_op jit(solution)/shard_map/all_to_all | solution.py:37
  184.9 6.7 %all-to-all-done.5 = f32[32,1,64]{2,1,0:T(1,128)S(1)} async-done(((f32[32,1,64]{2,1,0:T(1,128)}), f32[32,1,64]{2,1,0:T(1,128)S(1)}, u32[]{:S(2)}, u32[]{:S(2)}) %all-to-all-start.5) | async-done | bytes 8224 | tf_op jit(solution)/shard_map/all_to_all | solution.py:37
  193.0 3.9 %collective-permute-start.28 = (bf16[1,64,256]{2,1,0:T(8,128)(2,1)S(1)}, bf16[1,64,256]{2,1,0:T(8,128)(2,1)S(1)}, u32[]{:S(2)}, u32[]{:S(2)}) collective-permute-start(bf16[1,64,256]{2,1,0:T(8,128)(2,1)S(1)} %bitcast.164), channel_id=1, source_target_pairs={{0,134},{1,135},{2,132},{3,133},{4,130},{5,131},{6,128},{7,129},{1... | collective-permute-start | bytes 98312 | tf_op jit(solution)/shard_map/ppermute | solution.py:29
  212.5 4.0 %collective-permute-done.18 = bf16[1,64,256]{2,1,0:T(8,128)(2,1)S(1)} collective-permute-done((bf16[1,64,256]{2,1,0:T(8,128)(2,1)S(1)}, bf16[1,64,256]{2,1,0:T(8,128)(2,1)S(1)}, u32[]{:S(2)}, u32[]{:S(2)}) %collective-permute-start.18) | collective-permute-done | bytes 32800 | tf_op jit(solution)/shard_map/ppermute | solution.py:29
  216.5 5.7 %collective-permute-done.19 = bf16[1,64,256]{2,1,0:T(8,128)(2,1)S(1)} collective-permute-done((bf16[1,64,256]{2,1,0:T(8,128)(2,1)S(1)}, bf16[1,64,256]{2,1,0:T(8,128)(2,1)S(1)}, u32[]{:S(2)}, u32[]{:S(2)}) %collective-permute-start.19) | collective-permute-done | bytes 32800 | tf_op jit(solution)/shard_map/ppermute | solution.py:29
  231.1 7.3 %collective-permute-start.22 = (bf16[1,64,256]{2,1,0:T(8,128)(2,1)S(1)}, bf16[1,64,256]{2,1,0:T(8,128)(2,1)S(1)}, u32[]{:S(2)}, u32[]{:S(2)}) collective-permute-start(bf16[1,64,256]{2,1,0:T(8,128)(2,1)S(1)} %bitcast.173), channel_id=1, source_target_pairs={{0,128},{1,129},{2,130},{3,131},{4,132},{5,133},{6,134},{7,135},{1... | collective-permute-start | bytes 98312 | tf_op jit(solution)/shard_map/ppermute | solution.py:29
  244.3 4.2 %collective-permute-done.24 = bf16[1,64,256]{2,1,0:T(8,128)(2,1)S(1)} collective-permute-done((bf16[1,64,256]{2,1,0:T(8,128)(2,1)S(1)}, bf16[1,64,256]{2,1,0:T(8,128)(2,1)S(1)}, u32[]{:S(2)}, u32[]{:S(2)}) %collective-permute-start.24) | collective-permute-done | bytes 32800 | tf_op jit(solution)/shard_map/ppermute | solution.py:29
  255.1 5.2 %convolution_convert_fusion = bf16[256,7168]{1,0:T(8,128)(2,1)S(1)} fusion(bf16[512,7168]{1,0:T(8,128)(2,1)} %all-gather.5.cloned.1.call-done, bf16[512,512]{1,0:T(8,128)(2,1)S(1)} %bitcast.154, s32[]{:T(128)S(6)} %select_n.47), kind=kOutput, calls=%fused_computation.6 | convolution fusion | flops 1880883200 | bytes 11272196 | tf_op jit(solution)/shard_map/dot_general | solution.py:184
  260.2 47.3 %all_to_all.57 = bf16[16,16,7168]{2,1,0:T(8,128)(2,1)S(1)} all-to-all(bf16[16,16,7168]{2,1,0:T(8,128)(2,1)S(1)} %bitcast.142), channel_id=1, replica_groups=mesh['group'=2,'dp'=16,'tensor'=8] {'dp'}, dimensions={0} | all-to-all | bytes 7340032 | tf_op jit(solution)/shard_map/all_to_all | solution.py:60
  308.3 27.2 %all_to_all.58 = bf16[16,16,3584]{2,1,0:T(8,128)(2,1)S(1)} all-to-all(bf16[16,16,3584]{2,1,0:T(8,128)(2,1)S(1)} %broadcast_in_dim.43), channel_id=1, replica_groups=mesh['group'=2,'dp'=16,'tensor'=8] {'dp'}, dimensions={0} | all-to-all | bytes 3670016 | tf_op jit(solution)/shard_map/all_to_all | solution.py:47
  335.9 8.8 %all_to_all.59 = bf16[2,16,16,3584]{3,2,1,0:T(8,128)(2,1)S(1)} all-to-all(bf16[2,16,16,3584]{3,2,1,0:T(8,128)(2,1)S(1)} %broadcast_in_dim.44), channel_id=1, replica_groups=mesh['group'=2,'dp'=16,'tensor'=8] {'group'}, dimensions={0} | all-to-all | bytes 7340032 | tf_op jit(solution)/shard_map/all_to_all | solution.py:51
  345.8 19.4 %all_to_all.60 = f32[8,64,256]{2,1,0:T(8,128)S(1)} all-to-all(f32[8,64,256]{2,1,0:T(8,128)S(1)} %fusion), channel_id=1, replica_groups=mesh['group'=2,'dp'=16,'tensor'=8] {'tensor'}, dimensions={0} | all-to-all | bytes 1048576 | tf_op jit(solution)/shard_map/all_to_all | solution.py:85
  (170 shorter events, 115.0 us)
Async XLA Ops:
  6.5 94.5 %all-gather.3.cloned.1.call-start = ((), (), s32[]{:S(2)}) async-start(), calls=%async_computation.10 | async-start | bytes 1966080 | tf_op jit(solution)/shard_map/all_gather | solution.py:79
  8.8 68.8 %collective-permute-start.14 = (bf16[1,66,256]{2,1,0:T(8,128)(2,1)S(1)}, bf16[1,66,256]{2,1,0:T(8,128)(2,1)S(1)}, u32[]{:S(2)}, u32[]{:S(2)}) collective-permute-start(bf16[1,66,256]{2,1,0:T(8,128)(2,1)S(1)} %fusion.14), channel_id=1, source_target_pairs={{0,135},{1,134},{2,133},{3,132},{4,131},{5,130},{6,129},{7,128},{1... | collective-permute-start | bytes 101384 | tf_op jit(solution)/shard_map/ppermute | solution.py:29
  15.8 61.8 %collective-permute-start.13 = (bf16[1,66,256]{2,1,0:T(8,128)(2,1)S(1)}, bf16[1,66,256]{2,1,0:T(8,128)(2,1)S(1)}, u32[]{:S(2)}, u32[]{:S(2)}) collective-permute-start(bf16[1,66,256]{2,1,0:T(8,128)(2,1)S(1)} %fusion.14), channel_id=1, source_target_pairs={{0,134},{1,135},{2,132},{3,133},{4,130},{5,131},{6,128},{7,129},{1... | collective-permute-start | bytes 101384 | tf_op jit(solution)/shard_map/ppermute | solution.py:29
  16.3 61.3 %collective-permute-start.12 = (bf16[1,66,256]{2,1,0:T(8,128)(2,1)S(1)}, bf16[1,66,256]{2,1,0:T(8,128)(2,1)S(1)}, u32[]{:S(2)}, u32[]{:S(2)}) collective-permute-start(bf16[1,66,256]{2,1,0:T(8,128)(2,1)S(1)} %fusion.14), channel_id=1, source_target_pairs={{0,133},{1,132},{2,135},{3,134},{4,129},{5,128},{6,131},{7,130},{1... | collective-permute-start | bytes 101384 | tf_op jit(solution)/shard_map/ppermute | solution.py:29
  20.1 57.5 %collective-permute-start.11 = (bf16[1,66,256]{2,1,0:T(8,128)(2,1)S(1)}, bf16[1,66,256]{2,1,0:T(8,128)(2,1)S(1)}, u32[]{:S(2)}, u32[]{:S(2)}) collective-permute-start(bf16[1,66,256]{2,1,0:T(8,128)(2,1)S(1)} %fusion.14), channel_id=1, source_target_pairs={{0,132},{1,133},{2,134},{3,135},{4,128},{5,129},{6,130},{7,131},{1... | collective-permute-start | bytes 101384 | tf_op jit(solution)/shard_map/ppermute | solution.py:29
  35.0 7.0 %collective-permute-start.3 = (bf16[1,66,256]{2,1,0:T(8,128)(2,1)S(1)}, bf16[1,66,256]{2,1,0:T(8,128)(2,1)S(1)}, u32[]{:S(2)}, u32[]{:S(2)}) collective-permute-start(bf16[1,66,256]{2,1,0:T(8,128)(2,1)S(1)} %fusion.14), channel_id=1, source_target_pairs={{0,4},{1,5},{2,6},{3,7},{4,0},{5,1},{6,2},{7,3},{128,132},{129,133... | collective-permute-start | bytes 101384 | tf_op jit(solution)/shard_map/ppermute | solution.py:29
  42.1 5.9 %collective-permute-start.4 = (bf16[1,66,256]{2,1,0:T(8,128)(2,1)S(1)}, bf16[1,66,256]{2,1,0:T(8,128)(2,1)S(1)}, u32[]{:S(2)}, u32[]{:S(2)}) collective-permute-start(bf16[1,66,256]{2,1,0:T(8,128)(2,1)S(1)} %fusion.14), channel_id=1, source_target_pairs={{0,5},{1,4},{2,7},{3,6},{4,1},{5,0},{6,3},{7,2},{128,133},{129,132... | collective-permute-start | bytes 101384 | tf_op jit(solution)/shard_map/ppermute | solution.py:29
  57.3 7.3 %collective-permute-start.7 = (bf16[1,66,256]{2,1,0:T(8,128)(2,1)S(1)}, bf16[1,66,256]{2,1,0:T(8,128)(2,1)S(1)}, u32[]{:S(2)}, u32[]{:S(2)}) collective-permute-start(bf16[1,66,256]{2,1,0:T(8,128)(2,1)S(1)} %fusion.14), channel_id=1, source_target_pairs={{0,128},{1,129},{2,130},{3,131},{4,132},{5,133},{6,134},{7,135},{1... | collective-permute-start | bytes 101384 | tf_op jit(solution)/shard_map/ppermute | solution.py:29
  72.4 5.2 %collective-permute-start.10 = (bf16[1,66,256]{2,1,0:T(8,128)(2,1)S(1)}, bf16[1,66,256]{2,1,0:T(8,128)(2,1)S(1)}, u32[]{:S(2)}, u32[]{:S(2)}) collective-permute-start(bf16[1,66,256]{2,1,0:T(8,128)(2,1)S(1)} %fusion.14), channel_id=1, source_target_pairs={{0,131},{1,130},{2,129},{3,128},{4,135},{5,134},{6,133},{7,132},{1... | collective-permute-start | bytes 101384 | tf_op jit(solution)/shard_map/ppermute | solution.py:29
  82.1 13.2 %all-to-all-start = ((f32[16,1,544]{2,1,0:T(1,128)}), f32[16,1,544]{2,1,0:T(1,128)S(1)}, u32[]{:S(2)}, u32[]{:S(2)}) async-start(f32[16,1,544]{2,1,0:T(1,128)} %broadcast_in_dim.36), calls=%async_computation | async-start | bytes 81920 | tf_op jit(solution)/shard_map/all_to_all | solution.py:157
  104.0 21.8 %all-to-all-start.1 = ((f32[16,16,1280]{2,1,0:T(8,128)}), f32[16,16,1280]{2,1,0:T(8,128)S(1)}, u32[]{:S(2)}, u32[]{:S(2)}) async-start(f32[16,16,1280]{2,1,0:T(8,128)} %bitcast.26), calls=%async_computation.1 | async-start | bytes 2621440 | tf_op jit(solution)/shard_map/all_to_all | solution.py:60
  107.7 147.4 %all-gather.5.cloned.1.call-start = ((), (), s32[]{:S(2)}) async-start(), calls=%async_computation.11 | async-start | bytes 11010048 | tf_op jit(solution)/shard_map/all_gather | solution.py:79
  130.7 13.8 %all-to-all-start.2 = ((bf16[16,16,1024]{2,1,0:T(8,128)(2,1)}), bf16[16,16,1024]{2,1,0:T(8,128)(2,1)S(1)}, u32[]{:S(2)}, u32[]{:S(2)}) async-start(bf16[16,16,1024]{2,1,0:T(8,128)(2,1)} %broadcast_in_dim.40), calls=%async_computation.2 | async-start | bytes 1048576 | tf_op jit(solution)/shard_map/all_to_all | solution.py:47
  179.6 12.1 %all-to-all-start.5 = ((f32[32,1,64]{2,1,0:T(1,128)}), f32[32,1,64]{2,1,0:T(1,128)S(1)}, u32[]{:S(2)}, u32[]{:S(2)}) async-start(f32[32,1,64]{2,1,0:T(1,128)} %broadcast_in_dim.42), calls=%async_computation.5 | async-start | bytes 32768 | tf_op jit(solution)/shard_map/all_to_all | solution.py:37
  191.8 9.0 %collective-permute-start.15 = (bf16[1,64,256]{2,1,0:T(8,128)(2,1)S(1)}, bf16[1,64,256]{2,1,0:T(8,128)(2,1)S(1)}, u32[]{:S(2)}, u32[]{:S(2)}) collective-permute-start(bf16[1,64,256]{2,1,0:T(8,128)(2,1)S(1)} %bitcast.162), channel_id=1, source_target_pairs={{0,1},{1,0},{2,3},{3,2},{4,5},{5,4},{6,7},{7,6},{128,129},{129,128... | collective-permute-start | bytes 98312 | tf_op jit(solution)/shard_map/ppermute | solution.py:29
  192.2 61.6 %collective-permute-start.29 = (bf16[1,64,256]{2,1,0:T(8,128)(2,1)S(1)}, bf16[1,64,256]{2,1,0:T(8,128)(2,1)S(1)}, u32[]{:S(2)}, u32[]{:S(2)}) collective-permute-start(bf16[1,64,256]{2,1,0:T(8,128)(2,1)S(1)} %bitcast.163), channel_id=1, source_target_pairs={{0,135},{1,134},{2,133},{3,132},{4,131},{5,130},{6,129},{7,128},{1... | collective-permute-start | bytes 98312 | tf_op jit(solution)/shard_map/ppermute | solution.py:29
  193.0 60.7 %collective-permute-start.28 = (bf16[1,64,256]{2,1,0:T(8,128)(2,1)S(1)}, bf16[1,64,256]{2,1,0:T(8,128)(2,1)S(1)}, u32[]{:S(2)}, u32[]{:S(2)}) collective-permute-start(bf16[1,64,256]{2,1,0:T(8,128)(2,1)S(1)} %bitcast.164), channel_id=1, source_target_pairs={{0,134},{1,135},{2,132},{3,133},{4,130},{5,131},{6,128},{7,129},{1... | collective-permute-start | bytes 98312 | tf_op jit(solution)/shard_map/ppermute | solution.py:29
  196.9 56.8 %collective-permute-start.27 = (bf16[1,64,256]{2,1,0:T(8,128)(2,1)S(1)}, bf16[1,64,256]{2,1,0:T(8,128)(2,1)S(1)}, u32[]{:S(2)}, u32[]{:S(2)}) collective-permute-start(bf16[1,64,256]{2,1,0:T(8,128)(2,1)S(1)} %bitcast.165), channel_id=1, source_target_pairs={{0,133},{1,132},{2,135},{3,134},{4,129},{5,128},{6,131},{7,130},{1... | collective-permute-start | bytes 98312 | tf_op jit(solution)/shard_map/ppermute | solution.py:29
  197.2 56.5 %collective-permute-start.26 = (bf16[1,64,256]{2,1,0:T(8,128)(2,1)S(1)}, bf16[1,64,256]{2,1,0:T(8,128)(2,1)S(1)}, u32[]{:S(2)}, u32[]{:S(2)}) collective-permute-start(bf16[1,64,256]{2,1,0:T(8,128)(2,1)S(1)} %bitcast.166), channel_id=1, source_target_pairs={{0,132},{1,133},{2,134},{3,135},{4,128},{5,129},{6,130},{7,131},{1... | collective-permute-start | bytes 98312 | tf_op jit(solution)/shard_map/ppermute | solution.py:29
  209.8 6.7 %collective-permute-start.18 = (bf16[1,64,256]{2,1,0:T(8,128)(2,1)S(1)}, bf16[1,64,256]{2,1,0:T(8,128)(2,1)S(1)}, u32[]{:S(2)}, u32[]{:S(2)}) collective-permute-start(bf16[1,64,256]{2,1,0:T(8,128)(2,1)S(1)} %bitcast.169), channel_id=1, source_target_pairs={{0,4},{1,5},{2,6},{3,7},{4,0},{5,1},{6,2},{7,3},{128,132},{129,133... | collective-permute-start | bytes 98312 | tf_op jit(solution)/shard_map/ppermute | solution.py:29
  216.5 5.8 %collective-permute-start.19 = (bf16[1,64,256]{2,1,0:T(8,128)(2,1)S(1)}, bf16[1,64,256]{2,1,0:T(8,128)(2,1)S(1)}, u32[]{:S(2)}, u32[]{:S(2)}) collective-permute-start(bf16[1,64,256]{2,1,0:T(8,128)(2,1)S(1)} %bitcast.170), channel_id=1, source_target_pairs={{0,5},{1,4},{2,7},{3,6},{4,1},{5,0},{6,3},{7,2},{128,133},{129,132... | collective-permute-start | bytes 98312 | tf_op jit(solution)/shard_map/ppermute | solution.py:29
  231.1 8.2 %collective-permute-start.22 = (bf16[1,64,256]{2,1,0:T(8,128)(2,1)S(1)}, bf16[1,64,256]{2,1,0:T(8,128)(2,1)S(1)}, u32[]{:S(2)}, u32[]{:S(2)}) collective-permute-start(bf16[1,64,256]{2,1,0:T(8,128)(2,1)S(1)} %bitcast.173), channel_id=1, source_target_pairs={{0,128},{1,129},{2,130},{3,131},{4,132},{5,133},{6,134},{7,135},{1... | collective-permute-start | bytes 98312 | tf_op jit(solution)/shard_map/ppermute | solution.py:29
  239.3 5.1 %collective-permute-start.23 = (bf16[1,64,256]{2,1,0:T(8,128)(2,1)S(1)}, bf16[1,64,256]{2,1,0:T(8,128)(2,1)S(1)}, u32[]{:S(2)}, u32[]{:S(2)}) collective-permute-start(bf16[1,64,256]{2,1,0:T(8,128)(2,1)S(1)} %bitcast.174), channel_id=1, source_target_pairs={{0,129},{1,128},{2,131},{3,130},{4,133},{5,132},{6,135},{7,134},{1... | collective-permute-start | bytes 98312 | tf_op jit(solution)/shard_map/ppermute | solution.py:29
  248.6 5.1 %collective-permute-start.25 = (bf16[1,64,256]{2,1,0:T(8,128)(2,1)S(1)}, bf16[1,64,256]{2,1,0:T(8,128)(2,1)S(1)}, u32[]{:S(2)}, u32[]{:S(2)}) collective-permute-start(bf16[1,64,256]{2,1,0:T(8,128)(2,1)S(1)} %bitcast.176), channel_id=1, source_target_pairs={{0,131},{1,130},{2,129},{3,128},{4,135},{5,134},{6,133},{7,132},{1... | collective-permute-start | bytes 98312 | tf_op jit(solution)/shard_map/ppermute | solution.py:29
  (17 other events, 466.8 us)
Sparse Core Ops, SparseCore 0:
  24.4 16.3 all-gather.2
  112.2 25.7 all-gather.4
